TPU v7x, 32 devices: a whole 2x2x4 slice. The times are simulated.
32 devices in a mesh: narrow: 8 (over z, x), wide: 4 (over y, core).
Axes of the slice: x: 2, y: 2, z: 4, core: 2. Of those that a mesh axis runs over, the one named last changes fastest.
Arguments:
- amps: bfloat16 [16, 512, 512], P(None, 'narrow', 'wide'), may hold values from -1 to 1
- left_fit: bfloat16 [64, 512, 256], P(None, 'narrow'), may hold values from -0.375 to 0.375
- right_fit: bfloat16 [512, 512, 256], P('narrow', 'wide'), may hold values from -0.375 to 0.375
- pair_list: int32 [16, 2], P('narrow'), may hold values from 0 to 127, as said below
- occ_energy: float32 [128], replicated, may hold values from -2 to -0.5
- vir_energy: float32 [512], replicated, may hold values from 0.5 to 3
Outputs:
- update: float32 [16, 64, 512], P('narrow', None, 'wide')
Inputs may be any that keep to these rules, and one draw needn't show every extreme that they name: `pair_list`: each row (i, j) has i <= j.
All inputs are finite; a program needn't handle non-finite values.
Results may differ from a plain program's by a relative error of at most 0.0029.
Values may be sent and summed in bfloat16 or wider, within the bound.
No kernel may reach another device: no remote copies, remote signals or barrier semaphores. Data moves between devices by JAX's collectives and lax.ppermute only.
A program may use at most 128 MiB of HBM per device.

v0:
```python
import jax
import jax.numpy as jnp
from jax import lax
from jax.sharding import PartitionSpec as P


def body(amps, left_fit, right_fit, pair_list, occ_energy, vir_energy):
    right_all = lax.all_gather(right_fit, "narrow", axis=0, tiled=True)
    vir_total, col_width, aux_width = right_all.shape
    right_mat = right_all.reshape(vir_total, col_width * aux_width)
    rows_total = left_fit.shape[0]
    amps_full = lax.all_to_all(amps, "narrow", split_axis=0, concat_axis=1, tiled=True)
    pairs_here = amps_full.shape[0]
    partials = []
    for start_row in range(0, rows_total, 16):
        row_block = left_fit[start_row : start_row + 16]
        running = jnp.einsum(
            "acq,pcd->padq",
            lax.all_gather(row_block, "narrow", axis=1, tiled=True),
            amps_full,
            preferred_element_type=jnp.float32,
        )
        rows_here = running.shape[1]
        mixed_rows = running.astype(jnp.bfloat16).reshape(
            pairs_here * rows_here, col_width * aux_width
        )
        project_ladder_part = lax.dot_general(
            mixed_rows, right_mat, (((1,), (1,)), ((), ())), preferred_element_type=jnp.float32
        )
        partials.append(project_ladder_part.reshape(pairs_here, rows_here, vir_total))
    reduced = [
        lax.psum_scatter(ladder_part, "wide", scatter_dimension=2, tiled=True)
        for ladder_part in partials
    ]
    ladder_sum = jnp.concatenate(reduced, axis=1)
    local_cols = ladder_sum.shape[2]
    occ_ids = jnp.arange(occ_energy.shape[0], dtype=jnp.int32)
    occ_first = jnp.sum(
        jnp.where(pair_list[:, 0:1] == occ_ids[None, :], occ_energy[None, :], 0.0), axis=1
    )
    occ_second = jnp.sum(
        jnp.where(pair_list[:, 1:2] == occ_ids[None, :], occ_energy[None, :], 0.0), axis=1
    )
    vir_cols = lax.dynamic_slice_in_dim(
        vir_energy, lax.axis_index("wide") * local_cols, local_cols, 0
    )
    vir_rows = vir_energy[:rows_total]
    denominator = (
        (occ_first + occ_second)[:, None, None] - vir_rows[None, :, None] - vir_cols[None, None, :]
    )
    return ladder_sum / denominator


def solution(mesh):
    return jax.shard_map(
        body,
        mesh=mesh,
        in_specs=(
            P(None, "narrow", "wide"),
            P(None, "narrow", None),
            P("narrow", "wide", None),
            P("narrow", None),
            P(),
            P(),
        ),
        out_specs=P("narrow", None, "wide"),
        check_vma=False,
    )
```

profile of v0, /device:TPU:0, one launch (start us, length us, event | category | flops | bytes accessed | tf_op | source)
XLA Modules:
  0.0 1060.1 jit_solution(1422802223781420822)
XLA Ops:
  6.5 0.0 all-gather.14.cloned.1.call-start
  6.5 2.9 fusion.50
  9.4 0.0 all-gather.14.cloned.1.call-update
  9.5 0.0 all-gather.12.cloned.1.call-start
  9.5 0.7 all-gather.12.cloned.1.call-update
  10.2 0.0 all-gather.10.cloned.1.call-start
  10.3 0.7 all-gather.10.cloned.1.call-update
  11.0 0.0 all-gather.6.cloned.1.call-start
  11.0 0.5 all-gather.6.cloned.1.call-update
  11.5 0.0 all-gather.8.cloned.1.call-start
  11.6 6.5 copy.21
  18.1 0.0 copy-start.2
  18.1 0.0 all-gather.8.cloned.1.call-update
  18.1 7.4 all-to-all-start
  25.5 0.0 reduce-scatter.11.cloned.1.call-start
  25.6 0.0 copy-done.2
  25.6 0.1 dynamic_slice.3
  25.7 0.0 copy-done
  25.7 0.2 slice_reduce_fusion
  25.8 0.0 copy-done.1
  25.8 0.2 fusion.49
  26.1 16.1 %all-to-all-done = bf16[16,64,128]{2,1,0:T(8,128)(2,1)S(1)} async-done(((bf16[16,64,128]{2,1,0:T(8,128)(2,1)}), bf16[16,64,128]{2,1,0:T(8,128)(2,1)S(1)}, u32[]{:S(2)}, u32[]{:S(2)}) %all-to-all-start) | async-done | bytes 262176 | tf_op jit(solution)/shard_map/all_to_all | solution.py:12
  42.2 49.1 %all-gather.14.cloned.1.call-done = bf16[16,512,256]{2,1,0:T(8,128)(2,1)} async-done(((bf16[16,64,256]{2,1,0:T(8,128)(2,1)}), bf16[16,512,256]{2,1,0:T(8,128)(2,1)}) %all-gather.14.cloned.1.call-update) | async-done | bytes 4194320 | tf_op jit(solution)/shard_map/all_gather | solution.py:19
  91.2 4.8 convert_bitcast_fusion
  96.0 69.1 %all-gather.12.cloned.1.call-done = bf16[16,512,256]{2,1,0:T(8,128)(2,1)} async-done(((bf16[16,64,256]{2,1,0:T(8,128)(2,1)}), bf16[16,512,256]{2,1,0:T(8,128)(2,1)}) %all-gather.12.cloned.1.call-update) | async-done | bytes 4194320 | tf_op jit(solution)/shard_map/all_gather | solution.py:19
  165.1 4.8 convert_bitcast_fusion.1
  169.9 69.1 %all-gather.10.cloned.1.call-done = bf16[16,512,256]{2,1,0:T(8,128)(2,1)} async-done(((bf16[16,64,256]{2,1,0:T(8,128)(2,1)}), bf16[16,512,256]{2,1,0:T(8,128)(2,1)}) %all-gather.10.cloned.1.call-update) | async-done | bytes 4194320 | tf_op jit(solution)/shard_map/all_gather | solution.py:19
  239.0 4.9 convert_bitcast_fusion.2
  243.8 68.9 %all-gather.6.cloned.1.call-done = bf16[16,512,256]{2,1,0:T(8,128)(2,1)} async-done(((bf16[16,64,256]{2,1,0:T(8,128)(2,1)}), bf16[16,512,256]{2,1,0:T(8,128)(2,1)}) %all-gather.6.cloned.1.call-update) | async-done | bytes 4194320 | tf_op jit(solution)/shard_map/all_gather | solution.py:19
  312.7 3.5 convert_bitcast_fusion.3
  316.2 634.0 %all-gather.8.cloned.1.call-done = bf16[512,128,256]{2,0,1:T(8,128)(2,1)} async-done(((bf16[64,128,256]{2,0,1:T(8,128)(2,1)}), bf16[512,128,256]{2,0,1:T(8,128)(2,1)}) %all-gather.8.cloned.1.call-update) | async-done | bytes 33554448 | tf_op jit(solution)/shard_map/all_gather | solution.py:8
  950.1 16.3 %fusion.43 = f32[2,16,512]{2,1,0:T(8,128)} fusion(bf16[512,128,256]{2,0,1:T(8,128)(2,1)} %all-gather.8.cloned.1.call-done, bf16[2,16,128,256]{3,2,1,0:T(8,128)(2,1)} %convert_bitcast_fusion), kind=kOutput, calls=%fused_computation.27 | convolution fusion | flops 1073741824 | bytes 35717120 | tf_op jit(solution)/shard_map/dot_general | solution.py:27
  966.4 0.0 reduce-scatter.11.cloned.1.call-update
  966.4 0.0 reduce-scatter.9.cloned.1.call-start
  966.5 16.3 %fusion.38 = f32[2,16,512]{2,1,0:T(8,128)} fusion(bf16[512,128,256]{2,0,1:T(8,128)(2,1)} %all-gather.8.cloned.1.call-done, bf16[2,16,128,256]{3,2,1,0:T(8,128)(2,1)} %convert_bitcast_fusion.1), kind=kOutput, calls=%fused_computation.26 | convolution fusion | flops 1073741824 | bytes 35717120 | tf_op jit(solution)/shard_map/dot_general | solution.py:27
  982.8 0.0 reduce-scatter.9.cloned.1.call-update
  982.8 0.2 reduce-scatter.7.cloned.1.call-start
  983.0 16.3 %fusion.33 = f32[2,16,512]{2,1,0:T(8,128)} fusion(bf16[512,128,256]{2,0,1:T(8,128)(2,1)} %all-gather.8.cloned.1.call-done, bf16[2,16,128,256]{3,2,1,0:T(8,128)(2,1)} %convert_bitcast_fusion.2), kind=kOutput, calls=%fused_computation.25 | convolution fusion | flops 1073741824 | bytes 35717120 | tf_op jit(solution)/shard_map/dot_general | solution.py:27
  999.4 0.0 reduce-scatter.7.cloned.1.call-update
  999.4 0.0 slice-start
  999.4 0.0 reduce-scatter.5.cloned.1.call-start
  999.4 15.9 %fusion.28 = f32[2,16,512]{2,1,0:T(8,128)} fusion(bf16[512,128,256]{2,0,1:T(8,128)(2,1)} %all-gather.8.cloned.1.call-done, bf16[2,16,128,256]{3,2,1,0:T(8,128)(2,1)S(1)} %convert_bitcast_fusion.3), kind=kOutput, calls=%fused_computation.24 | convolution fusion | flops 1073741824 | bytes 35717120 | tf_op jit(solution)/shard_map/dot_general | solution.py:27
  1015.3 0.0 reduce-scatter.5.cloned.1.call-update
  1015.4 0.0 slice-done
  1015.4 0.1 broadcast_subtract_fusion
  1015.5 14.6 %reduce-scatter.7.cloned.1.call-done = f32[2,16,128]{2,1,0:T(8,128)} async-done(((f32[2,16,512]{2,1,0:T(8,128)}), f32[2,16,128]{2,1,0:T(8,128)}) %reduce-scatter.7.cloned.1.call-update) | async-done | bytes 16400 | tf_op jit(solution)/shard_map/reduce_scatter | solution.py:32
  1030.0 22.0 %reduce-scatter.5.cloned.1.call-done = f32[2,16,128]{2,1,0:T(8,128)} async-done(((f32[2,16,512]{2,1,0:T(8,128)}), f32[2,16,128]{2,1,0:T(8,128)}) %reduce-scatter.5.cloned.1.call-update) | async-done | bytes 16400 | tf_op jit(solution)/shard_map/reduce_scatter | solution.py:32
  1052.1 1.5 maximum_divide_fusion
  (6 shorter events, 0.0 us)
Async XLA Ops:
  6.5 84.7 %all-gather.14.cloned.1.call-start = ((), (), s32[]{:S(2)}) async-start(), calls=%async_computation.12 | async-start | bytes 4718592 | tf_op jit(solution)/shard_map/all_gather | solution.py:19
  9.5 155.6 %all-gather.12.cloned.1.call-start = ((), (), s32[]{:S(2)}) async-start(), calls=%async_computation.10 | async-start | bytes 4718592 | tf_op jit(solution)/shard_map/all_gather | solution.py:19
  10.2 228.8 %all-gather.10.cloned.1.call-start = ((), (), s32[]{:S(2)}) async-start(), calls=%async_computation.8 | async-start | bytes 4718592 | tf_op jit(solution)/shard_map/all_gather | solution.py:19
  11.0 301.7 %all-gather.6.cloned.1.call-start = ((), (), s32[]{:S(2)}) async-start(), calls=%async_computation.5 | async-start | bytes 4718592 | tf_op jit(solution)/shard_map/all_gather | solution.py:19
  11.5 938.6 %all-gather.8.cloned.1.call-start = ((), (), s32[]{:S(2)}) async-start(), calls=%async_computation.6 | async-start | bytes 37748736 | tf_op jit(solution)/shard_map/all_gather | solution.py:8
  18.1 7.5 copy-start.2
  18.1 7.6 copy-start
  18.1 7.7 copy-start.1
  18.1 24.0 %all-to-all-start = ((bf16[16,64,128]{2,1,0:T(8,128)(2,1)}), bf16[16,64,128]{2,1,0:T(8,128)(2,1)S(1)}, u32[]{:S(2)}, u32[]{:S(2)}) async-start(bf16[16,64,128]{2,1,0:T(8,128)(2,1)} %param.6), calls=%async_computation | async-start | bytes 524288 | tf_op jit(solution)/shard_map/all_to_all | solution.py:12
  25.5 989.9 %reduce-scatter.11.cloned.1.call-start = ((), (), s32[]{:S(2)}) async-start(), calls=%async_computation.13 | async-start | bytes 81920 | tf_op jit(solution)/shard_map/reduce_scatter | solution.py:32
  966.4 49.0 %reduce-scatter.9.cloned.1.call-start = ((), (), s32[]{:S(2)}) async-start(), calls=%async_computation.11 | async-start | bytes 81920 | tf_op jit(solution)/shard_map/reduce_scatter | solution.py:32
  982.8 47.2 %reduce-scatter.7.cloned.1.call-start = ((), (), s32[]{:S(2)}) async-start(), calls=%async_computation.9 | async-start | bytes 81920 | tf_op jit(solution)/shard_map/reduce_scatter | solution.py:32
  999.4 16.0 %slice-start = ((f32[512]{0:T(512)}), f32[64]{0:T(128)S(1)}, s32[]{:S(2)}) async-start(f32[512]{0:T(512)} %param.11), calls=%async_computation.14 | async-start | bytes 1024 | tf_op jit(solution)/shard_map/slice | solution.py:47
  999.4 52.7 %reduce-scatter.5.cloned.1.call-start = ((), (), s32[]{:S(2)}) async-start(), calls=%async_computation.7 | async-start | bytes 81920 | tf_op jit(solution)/shard_map/reduce_scatter | solution.py:32
Sparse Core Ops, SparseCore 0:
  9.6 81.6 all-gather.13
  93.4 71.6 all-gather.11
  167.3 71.6 all-gather.9
  241.0 71.6 all-gather.5
  314.1 635.9 all-gather.7
  966.5 19.4 reduce-scatter.10
  988.6 19.4 reduce-scatter.8
  1010.5 19.5 reduce-scatter.6
  1032.6 19.4 reduce-scatter.4
where the time goes:
time: 1060 us
  waiting for transfers between devices  945 us (89%)
  matrix products  82.7 us (8%)
  between operations  13.3 us (1%)
    all_gather x1, waiting for transfers between devices, body(): right_all = lax.all_gather(right_fit, 'narrow', axis=0, tiled=True)  634 us
    all_gather x4, waiting for transfers between devices, body(): lax.all_gather(row_block, 'narrow', axis=1, tiled=True)  256 us
    dot_general x4, matrix products, body(): lax.dot_general(mixed_rows, right_mat, (((1,), (1,)), ((), ())), preferre...  64.8 us
    reduce_scatter x4, waiting for transfers between devices, body(): lax.psum_scatter(ladder_part, 'wide', scatter_dimension=2, tiled=True)  36.6 us
  transfers between devices with their start and end apart: 10, of which 8 were waited for; matrix products, arithmetic and copies ran while one was open for 7% of the time, Pallas kernels for 0%

commit v1 on v0

--- a/solution.py
+++ b/solution.py
@@ -2,6 +2,27 @@
 import jax.numpy as jnp
 from jax import lax
 from jax.sharding import PartitionSpec as P
+
+
+def ring_gather(x, axis, dim):
+    size, here, rows = (lax.axis_size(axis), lax.axis_index(axis), x.shape[dim])
+    right = [(i, (i + 1) % size) for i in range(size)]
+    left = [(i, (i - 1) % size) for i in range(size)]
+    whole = jnp.zeros((*x.shape[:dim], size * rows, *x.shape[dim + 1 :]), x.dtype)
+    whole = lax.dynamic_update_slice_in_dim(whole, x, here * rows, axis=dim)
+    from_left = from_right = x
+    halfway = size // 2
+    for step in range(1, halfway + 1):
+        from_left = lax.ppermute(from_left, axis, right)
+        whole = lax.dynamic_update_slice_in_dim(
+            whole, from_left, (here - step) % size * rows, axis=dim
+        )
+        if step < size - halfway:
+            from_right = lax.ppermute(from_right, axis, left)
+            whole = lax.dynamic_update_slice_in_dim(
+                whole, from_right, (here + step) % size * rows, axis=dim
+            )
+    return whole
 
 
 def body(amps, left_fit, right_fit, pair_list, occ_energy, vir_energy):
@@ -16,7 +37,7 @@
         row_block = left_fit[start_row : start_row + 16]
         running = jnp.einsum(
             "acq,pcd->padq",
-            lax.all_gather(row_block, "narrow", axis=1, tiled=True),
+            ring_gather(row_block, "narrow", 1),
             amps_full,
             preferred_element_type=jnp.float32,
         )

time: 1060 us -> 1150 us (1.085)
  local copies, waits for them, and re-layouts: 9.72 us -> 421 us
  waiting for transfers between devices: 945 us -> 573 us
  starting transfers between devices: 7.9 us -> 47.2 us
    all_gather x1, waiting for transfers between devices: 634 us -> 0.01 us  [body(): right_all = lax.all_gather(right_fit, 'narrow', axis=0, tiled=True)]
    ppermute x0 -> x28, waiting for transfers between devices: none -> 505 us  [the longest x16 408 us: ring_gather(): from_left = lax.ppermute(from_left, axis, right)]
    dynamic_update_slice x0 -> x32, local copies, waits for them, and re-layouts: none -> 355 us  [the longest x16 174 us: ring_gather(): lax.dynamic_update_slice_in_dim(whole, from_left, (here - step) % size *...]
    all_gather x4 -> x0, waiting for transfers between devices: 256 us -> none  [body(): lax.all_gather(row_block, 'narrow', axis=1, tiled=True)]
    ppermute x0 -> x28, starting transfers between devices: none -> 30.9 us  [the longest x12 18.8 us: ring_gather(): from_right = lax.ppermute(from_right, axis, left)]
    ppermute x0 -> x28, local copies, waits for them, and re-layouts: none -> 27 us  [the longest x16 17.1 us: ring_gather(): from_left = lax.ppermute(from_left, axis, right)]
    convert_element_type x0 -> x4, local copies, waits for them, and re-layouts: none -> 15.4 us  [body(): running.astype(jnp.bfloat16)]
  transfers between devices with their start and end apart: 10 -> 34, of which waited for: 8 -> 25; matrix products, arithmetic and copies ran while one was open for 7% -> 42% of each run, Pallas kernels for 0% -> 0%
where the time goes in v1:
time: 1150 us; the launch traced here: 1140 us
  waiting for transfers between devices  573 us (50%)
  local copies, waits for them, and re-layouts  421 us (37%)
  matrix products  81.9 us (7%)
  starting transfers between devices  47.2 us (4%)
  between operations  14 us (1%)
    ppermute x16, waiting for transfers between devices, ring_gather(): from_left = lax.ppermute(from_left, axis, right)  408 us
    dynamic_update_slice x16, local copies, waits for them, and re-layouts, ring_gather(): lax.dynamic_update_slice_in_dim(whole, from_left, (here - step) % size *...  174 us
    dynamic_update_slice x12, local copies, waits for them, and re-layouts, ring_gather(): lax.dynamic_update_slice_in_dim(whole, from_right, (here + step) % size *...  139 us
    ppermute x12, waiting for transfers between devices, ring_gather(): from_right = lax.ppermute(from_right, axis, left)  97.1 us
    dot_general x4, matrix products, body(): lax.dot_general(mixed_rows, right_mat, (((1,), (1,)), ((), ())), preferre...  64.2 us
    reduce_scatter x4, waiting for transfers between devices, body(): lax.psum_scatter(ladder_part, 'wide', scatter_dimension=2, tiled=True)  43.8 us
    dynamic_update_slice x4, local copies, waits for them, and re-layouts, ring_gather(): whole = lax.dynamic_update_slice_in_dim(whole, x, here * rows, axis=dim)  41.6 us
    all_to_all x1, waiting for transfers between devices, body(): lax.all_to_all(amps, 'narrow', split_axis=0, concat_axis=1, tiled=True)  23.8 us
  transfers between devices with their start and end apart: 34, of which 25 were waited for; matrix products, arithmetic and copies ran while one was open for 42% of the time, Pallas kernels for 0%

profile of v1, /device:TPU:0, one launch (start us, length us, event | category | flops | bytes accessed | tf_op | source)
XLA Modules:
  0.0 1139.0 jit_solution(15816928569361012489)
XLA Ops:
  25.9 87.0 %collective-permute-done = bf16[16,64,256]{2,1,0:T(8,128)(2,1)S(1)} collective-permute-done((bf16[16,64,256]{2,1,0:T(8,128)(2,1)S(1)}, bf16[16,64,256]{2,1,0:T(8,128)(2,1)S(1)}, u32[]{:S(2)}, u32[]{:S(2)}) %collective-permute-start) | collective-permute-done | bytes 524320 | tf_op jit(solution)/shard_map/ppermute | solution.py:16
  122.6 35.3 %collective-permute-done.7 = bf16[16,64,256]{2,1,0:T(8,128)(2,1)S(1)} collective-permute-done((bf16[16,64,256]{2,1,0:T(8,128)(2,1)S(1)}, bf16[16,64,256]{2,1,0:T(8,128)(2,1)S(1)}, u32[]{:S(2)}, u32[]{:S(2)}) %collective-permute-start.7) | collective-permute-done | bytes 524320 | tf_op jit(solution)/shard_map/ppermute | solution.py:16
  167.5 35.3 %collective-permute-done.14 = bf16[16,64,256]{2,1,0:T(8,128)(2,1)S(1)} collective-permute-done((bf16[16,64,256]{2,1,0:T(8,128)(2,1)S(1)}, bf16[16,64,256]{2,1,0:T(8,128)(2,1)S(1)}, u32[]{:S(2)}, u32[]{:S(2)}) %collective-permute-start.14) | collective-permute-done | bytes 524320 | tf_op jit(solution)/shard_map/ppermute | solution.py:16
  212.4 35.3 %collective-permute-done.21 = bf16[16,64,256]{2,1,0:T(8,128)(2,1)S(1)} collective-permute-done((bf16[16,64,256]{2,1,0:T(8,128)(2,1)S(1)}, bf16[16,64,256]{2,1,0:T(8,128)(2,1)S(1)}, u32[]{:S(2)}, u32[]{:S(2)}) %collective-permute-start.21) | collective-permute-done | bytes 524320 | tf_op jit(solution)/shard_map/ppermute | solution.py:16
  257.4 35.2 %collective-permute-done.2 = bf16[16,64,256]{2,1,0:T(8,128)(2,1)S(1)} collective-permute-done((bf16[16,64,256]{2,1,0:T(8,128)(2,1)S(1)}, bf16[16,64,256]{2,1,0:T(8,128)(2,1)S(1)}, u32[]{:S(2)}, u32[]{:S(2)}) %collective-permute-start.2) | collective-permute-done | bytes 524320 | tf_op jit(solution)/shard_map/ppermute | solution.py:16
  302.3 35.3 %collective-permute-done.9 = bf16[16,64,256]{2,1,0:T(8,128)(2,1)S(1)} collective-permute-done((bf16[16,64,256]{2,1,0:T(8,128)(2,1)S(1)}, bf16[16,64,256]{2,1,0:T(8,128)(2,1)S(1)}, u32[]{:S(2)}, u32[]{:S(2)}) %collective-permute-start.9) | collective-permute-done | bytes 524320 | tf_op jit(solution)/shard_map/ppermute | solution.py:16
  347.3 35.3 %collective-permute-done.16 = bf16[16,64,256]{2,1,0:T(8,128)(2,1)S(1)} collective-permute-done((bf16[16,64,256]{2,1,0:T(8,128)(2,1)S(1)}, bf16[16,64,256]{2,1,0:T(8,128)(2,1)S(1)}, u32[]{:S(2)}, u32[]{:S(2)}) %collective-permute-start.16) | collective-permute-done | bytes 524320 | tf_op jit(solution)/shard_map/ppermute | solution.py:16
  392.3 35.2 %collective-permute-done.23 = bf16[16,64,256]{2,1,0:T(8,128)(2,1)} collective-permute-done((bf16[16,64,256]{2,1,0:T(8,128)(2,1)S(1)}, bf16[16,64,256]{2,1,0:T(8,128)(2,1)}, u32[]{:S(2)}, u32[]{:S(2)}) %collective-permute-start.23) | collective-permute-done | bytes 524320 | tf_op jit(solution)/shard_map/ppermute | solution.py:16
  427.5 9.8 collective-permute-done.24
  437.3 29.6 %collective-permute-done.4 = bf16[16,64,256]{2,1,0:T(8,128)(2,1)} collective-permute-done((bf16[16,64,256]{2,1,0:T(8,128)(2,1)S(1)}, bf16[16,64,256]{2,1,0:T(8,128)(2,1)}, u32[]{:S(2)}, u32[]{:S(2)}) %collective-permute-start.4) | collective-permute-done | bytes 524320 | tf_op jit(solution)/shard_map/ppermute | solution.py:16
  482.1 29.7 %collective-permute-done.11 = bf16[16,64,256]{2,1,0:T(8,128)(2,1)} collective-permute-done((bf16[16,64,256]{2,1,0:T(8,128)(2,1)S(1)}, bf16[16,64,256]{2,1,0:T(8,128)(2,1)}, u32[]{:S(2)}, u32[]{:S(2)}) %collective-permute-start.11) | collective-permute-done | bytes 524320 | tf_op jit(solution)/shard_map/ppermute | solution.py:16
  527.8 16.1 %all-to-all-start = ((bf16[16,64,128]{2,1,0:T(8,128)(2,1)}), bf16[16,64,128]{2,1,0:T(8,128)(2,1)S(1)}, u32[]{:S(2)}, u32[]{:S(2)}) async-start(bf16[16,64,128]{2,1,0:T(8,128)(2,1)} %param.6), calls=%async_computation | async-start | bytes 524288 | tf_op jit(solution)/shard_map/all_to_all | solution.py:33
  544.0 15.3 %collective-permute-done.18 = bf16[16,64,256]{2,1,0:T(8,128)(2,1)} collective-permute-done((bf16[16,64,256]{2,1,0:T(8,128)(2,1)S(1)}, bf16[16,64,256]{2,1,0:T(8,128)(2,1)}, u32[]{:S(2)}, u32[]{:S(2)}) %collective-permute-start.18) | collective-permute-done | bytes 524320 | tf_op jit(solution)/shard_map/ppermute | solution.py:16
  568.6 10.8 dynamic_update_slice.96
  581.8 10.3 dynamic_update_slice.104
  594.5 10.2 dynamic_update_slice.112
  607.1 10.3 dynamic_update_slice.120
  617.7 23.8 %all-to-all-done = bf16[16,64,128]{2,1,0:T(8,128)(2,1)S(1)} async-done(((bf16[16,64,128]{2,1,0:T(8,128)(2,1)}), bf16[16,64,128]{2,1,0:T(8,128)(2,1)S(1)}, u32[]{:S(2)}, u32[]{:S(2)}) %all-to-all-start) | async-done | bytes 262176 | tf_op jit(solution)/shard_map/all_to_all | solution.py:33
  642.6 11.6 %dynamic_update_slice.97 = bf16[16,512,256]{1,2,0:T(8,128)(2,1)} dynamic-update-slice(bf16[16,512,256]{1,2,0:T(8,128)(2,1)} %dynamic_update_slice.96, bf16[16,64,256]{1,2,0:T(8,128)(2,1)S(1)} %copy.48, s32[]{:T(128)} %constant.97.clone.1, s32[]{:T(128)S(6)} %select_n.133, s32[]{:T(128)} %constant.97.clone.1) | dynamic-update-slice | bytes 1048580 | tf_op jit(solution)/shard_map/dynamic_update_slice | solution.py:17
  654.7 11.5 %dynamic_update_slice.105 = bf16[16,512,256]{1,2,0:T(8,128)(2,1)} dynamic-update-slice(bf16[16,512,256]{1,2,0:T(8,128)(2,1)} %dynamic_update_slice.104, bf16[16,64,256]{1,2,0:T(8,128)(2,1)S(1)} %copy.59, s32[]{:T(128)} %constant.97.clone.1, s32[]{:T(128)S(6)} %select_n.133, s32[]{:T(128)} %constant.97.clone.1) | dynamic-update-slice | bytes 1048580 | tf_op jit(solution)/shard_map/dynamic_update_slice | solution.py:17
  666.7 12.2 %dynamic_update_slice.98 = bf16[16,512,256]{1,2,0:T(8,128)(2,1)} dynamic-update-slice(bf16[16,512,256]{1,2,0:T(8,128)(2,1)} %dynamic_update_slice.97, bf16[16,64,256]{1,2,0:T(8,128)(2,1)S(1)} %copy.49, s32[]{:T(128)} %constant.97.clone.1, s32[]{:T(128)S(6)} %select_n.135, s32[]{:T(128)} %constant.97.clone.1) | dynamic-update-slice | bytes 1048580 | tf_op jit(solution)/shard_map/dynamic_update_slice | solution.py:22
  679.4 12.3 %dynamic_update_slice.106 = bf16[16,512,256]{1,2,0:T(8,128)(2,1)} dynamic-update-slice(bf16[16,512,256]{1,2,0:T(8,128)(2,1)} %dynamic_update_slice.105, bf16[16,64,256]{1,2,0:T(8,128)(2,1)S(1)} %copy.60, s32[]{:T(128)} %constant.97.clone.1, s32[]{:T(128)S(6)} %select_n.135, s32[]{:T(128)} %constant.97.clone.1) | dynamic-update-slice | bytes 1048580 | tf_op jit(solution)/shard_map/dynamic_update_slice | solution.py:22
  692.2 11.5 %dynamic_update_slice.113 = bf16[16,512,256]{1,2,0:T(8,128)(2,1)} dynamic-update-slice(bf16[16,512,256]{1,2,0:T(8,128)(2,1)} %dynamic_update_slice.112, bf16[16,64,256]{1,2,0:T(8,128)(2,1)S(1)} %copy.68, s32[]{:T(128)} %constant.97.clone.1, s32[]{:T(128)S(6)} %select_n.133, s32[]{:T(128)} %constant.97.clone.1) | dynamic-update-slice | bytes 1048580 | tf_op jit(solution)/shard_map/dynamic_update_slice | solution.py:17
  704.2 12.3 %dynamic_update_slice.114 = bf16[16,512,256]{1,2,0:T(8,128)(2,1)} dynamic-update-slice(bf16[16,512,256]{1,2,0:T(8,128)(2,1)} %dynamic_update_slice.113, bf16[16,64,256]{1,2,0:T(8,128)(2,1)S(1)} %copy.69, s32[]{:T(128)} %constant.97.clone.1, s32[]{:T(128)S(6)} %select_n.135, s32[]{:T(128)} %constant.97.clone.1) | dynamic-update-slice | bytes 1048580 | tf_op jit(solution)/shard_map/dynamic_update_slice | solution.py:22
  717.0 11.5 %dynamic_update_slice.121 = bf16[16,512,256]{1,2,0:T(8,128)(2,1)} dynamic-update-slice(bf16[16,512,256]{1,2,0:T(8,128)(2,1)} %dynamic_update_slice.120, bf16[16,64,256]{1,2,0:T(8,128)(2,1)S(1)} %copy.77, s32[]{:T(128)} %constant.97.clone.1, s32[]{:T(128)S(6)} %select_n.133, s32[]{:T(128)} %constant.97.clone.1) | dynamic-update-slice | bytes 1048580 | tf_op jit(solution)/shard_map/dynamic_update_slice | solution.py:17
  729.0 12.2 %dynamic_update_slice.122 = bf16[16,512,256]{1,2,0:T(8,128)(2,1)} dynamic-update-slice(bf16[16,512,256]{1,2,0:T(8,128)(2,1)} %dynamic_update_slice.121, bf16[16,64,256]{1,2,0:T(8,128)(2,1)S(1)} %copy.78, s32[]{:T(128)} %constant.97.clone.1, s32[]{:T(128)S(6)} %select_n.135, s32[]{:T(128)} %constant.97.clone.1) | dynamic-update-slice | bytes 1048580 | tf_op jit(solution)/shard_map/dynamic_update_slice | solution.py:22
  761.5 10.4 dynamic_update_slice.100
  772.4 10.2 dynamic_update_slice.108
  794.0 10.3 dynamic_update_slice.116
  816.7 10.3 dynamic_update_slice.124
  828.6 12.2 %dynamic_update_slice.101 = bf16[16,512,256]{1,2,0:T(8,128)(2,1)} dynamic-update-slice(bf16[16,512,256]{1,2,0:T(8,128)(2,1)} %dynamic_update_slice.100, bf16[16,64,256]{1,2,0:T(8,128)(2,1)S(1)} %copy.52, s32[]{:T(128)} %constant.97.clone.1, s32[]{:T(128)S(6)} %select_n.141, s32[]{:T(128)} %constant.97.clone.1) | dynamic-update-slice | bytes 1048580 | tf_op jit(solution)/shard_map/dynamic_update_slice | solution.py:17
  842.4 12.3 %dynamic_update_slice.109 = bf16[16,512,256]{1,2,0:T(8,128)(2,1)} dynamic-update-slice(bf16[16,512,256]{1,2,0:T(8,128)(2,1)} %dynamic_update_slice.108, bf16[16,64,256]{1,2,0:T(8,128)(2,1)S(1)} %copy.63, s32[]{:T(128)} %constant.97.clone.1, s32[]{:T(128)S(6)} %select_n.141, s32[]{:T(128)} %constant.97.clone.1) | dynamic-update-slice | bytes 1048580 | tf_op jit(solution)/shard_map/dynamic_update_slice | solution.py:17
  855.2 12.2 %dynamic_update_slice.102 = bf16[16,512,256]{1,2,0:T(8,128)(2,1)} dynamic-update-slice(bf16[16,512,256]{1,2,0:T(8,128)(2,1)} %dynamic_update_slice.101, bf16[16,64,256]{1,2,0:T(8,128)(2,1)S(1)} %copy.53, s32[]{:T(128)} %constant.97.clone.1, s32[]{:T(128)S(6)} %select_n.143, s32[]{:T(128)} %constant.97.clone.1) | dynamic-update-slice | bytes 1048580 | tf_op jit(solution)/shard_map/dynamic_update_slice | solution.py:22
  867.9 12.2 %dynamic_update_slice.110 = bf16[16,512,256]{1,2,0:T(8,128)(2,1)} dynamic-update-slice(bf16[16,512,256]{1,2,0:T(8,128)(2,1)} %dynamic_update_slice.109, bf16[16,64,256]{1,2,0:T(8,128)(2,1)S(1)} %copy.64, s32[]{:T(128)} %constant.97.clone.1, s32[]{:T(128)S(6)} %select_n.143, s32[]{:T(128)} %constant.97.clone.1) | dynamic-update-slice | bytes 1048580 | tf_op jit(solution)/shard_map/dynamic_update_slice | solution.py:22
  881.7 12.3 %dynamic_update_slice.117 = bf16[16,512,256]{1,2,0:T(8,128)(2,1)} dynamic-update-slice(bf16[16,512,256]{1,2,0:T(8,128)(2,1)} %dynamic_update_slice.116, bf16[16,64,256]{1,2,0:T(8,128)(2,1)S(1)} %copy.72, s32[]{:T(128)} %constant.97.clone.1, s32[]{:T(128)S(6)} %select_n.141, s32[]{:T(128)} %constant.97.clone.1) | dynamic-update-slice | bytes 1048580 | tf_op jit(solution)/shard_map/dynamic_update_slice | solution.py:17
  895.5 12.3 %dynamic_update_slice.118 = bf16[16,512,256]{1,2,0:T(8,128)(2,1)} dynamic-update-slice(bf16[16,512,256]{1,2,0:T(8,128)(2,1)} %dynamic_update_slice.117, bf16[16,64,256]{1,2,0:T(8,128)(2,1)S(1)} %copy.73, s32[]{:T(128)} %constant.97.clone.1, s32[]{:T(128)S(6)} %select_n.143, s32[]{:T(128)} %constant.97.clone.1) | dynamic-update-slice | bytes 1048580 | tf_op jit(solution)/shard_map/dynamic_update_slice | solution.py:22
  909.3 12.2 %dynamic_update_slice.125 = bf16[16,512,256]{1,2,0:T(8,128)(2,1)} dynamic-update-slice(bf16[16,512,256]{1,2,0:T(8,128)(2,1)} %dynamic_update_slice.124, bf16[16,64,256]{1,2,0:T(8,128)(2,1)S(1)} %copy.81, s32[]{:T(128)} %constant.97.clone.1, s32[]{:T(128)S(6)} %select_n.141, s32[]{:T(128)} %constant.97.clone.1) | dynamic-update-slice | bytes 1048580 | tf_op jit(solution)/shard_map/dynamic_update_slice | solution.py:17
  923.1 12.2 %dynamic_update_slice.126 = bf16[16,512,256]{1,2,0:T(8,128)(2,1)} dynamic-update-slice(bf16[16,512,256]{1,2,0:T(8,128)(2,1)} %dynamic_update_slice.125, bf16[16,64,256]{1,2,0:T(8,128)(2,1)S(1)} %copy.82, s32[]{:T(128)} %constant.97.clone.1, s32[]{:T(128)S(6)} %select_n.143, s32[]{:T(128)} %constant.97.clone.1) | dynamic-update-slice | bytes 1048580 | tf_op jit(solution)/shard_map/dynamic_update_slice | solution.py:22
  943.3 10.5 dynamic_update_slice.103
  958.8 10.3 dynamic_update_slice.111
  981.6 10.3 dynamic_update_slice.119
  1002.8 10.2 dynamic_update_slice.127
  1022.3 16.2 %fusion.24 = f32[2,16,512]{2,1,0:T(8,128)} fusion(bf16[2,16,128,256]{3,1,2,0:T(8,128)(2,1)} %copy.57, bf16[512,128,256]{2,0,1:T(8,128)(2,1)} %all-gather.2.cloned.1.call-done), kind=kOutput, calls=%fused_computation.20 | convolution fusion | flops 1073741824 | bytes 35717120 | tf_op jit(solution)/shard_map/dot_general | solution.py:48
  1038.5 16.0 %fusion.27 = f32[2,16,512]{2,1,0:T(8,128)} fusion(bf16[2,16,128,256]{3,1,2,0:T(8,128)(2,1)S(1)} %copy.66, bf16[512,128,256]{2,0,1:T(8,128)(2,1)} %all-gather.2.cloned.1.call-done), kind=kOutput, calls=%fused_computation.21 | convolution fusion | flops 1073741824 | bytes 35717120 | tf_op jit(solution)/shard_map/dot_general | solution.py:48
  1054.6 16.3 %fusion.30 = f32[2,16,512]{2,1,0:T(8,128)} fusion(bf16[2,16,128,256]{3,1,2,0:T(8,128)(2,1)} %copy.75, bf16[512,128,256]{2,0,1:T(8,128)(2,1)} %all-gather.2.cloned.1.call-done), kind=kOutput, calls=%fused_computation.22 | convolution fusion | flops 1073741824 | bytes 35717120 | tf_op jit(solution)/shard_map/dot_general | solution.py:48
  1071.0 15.8 %fusion.33 = f32[2,16,512]{2,1,0:T(8,128)} fusion(bf16[2,16,128,256]{3,1,2,0:T(8,128)(2,1)S(1)} %copy-done, bf16[512,128,256]{2,0,1:T(8,128)(2,1)} %all-gather.2.cloned.1.call-done), kind=kOutput, calls=%fused_computation.23 | convolution fusion | flops 1073741824 | bytes 35717120 | tf_op jit(solution)/shard_map/dot_general | solution.py:48
  1087.1 21.7 %reduce-scatter.9.cloned.1.call-done = f32[2,16,128]{2,1,0:T(8,128)} async-done(((f32[2,16,512]{2,1,0:T(8,128)}), f32[2,16,128]{2,1,0:T(8,128)}) %reduce-scatter.9.cloned.1.call-update) | async-done | bytes 16400 | tf_op jit(solution)/shard_map/reduce_scatter | solution.py:53
  1108.8 21.9 %reduce-scatter.11.cloned.1.call-done = f32[2,16,128]{2,1,0:T(8,128)} async-done(((f32[2,16,512]{2,1,0:T(8,128)}), f32[2,16,128]{2,1,0:T(8,128)}) %reduce-scatter.11.cloned.1.call-update) | async-done | bytes 16400 | tf_op jit(solution)/shard_map/reduce_scatter | solution.py:53
  (196 shorter events, 242.0 us)
Async XLA Ops:
  6.5 1015.8 %all-gather.2.cloned.1.call-start = ((), (), s32[]{:S(2)}) async-start(), calls=%async_computation.5 | async-start | bytes 37748736 | tf_op jit(solution)/shard_map/all_gather | solution.py:29
  13.2 548.7 %copy-start.37 = (s32[2,2]{1,0:T(2,128)S(1)}, s32[2,2]{1,0:T(2,128)}, u32[]{:S(2)}) copy-start(s32[2,2]{1,0:T(2,128)} %param.9) | copy-start | bytes 52
  15.0 242.4 %copy-start.4 = (bf16[16,64,256]{2,1,0:T(8,128)(2,1)}, bf16[16,64,256]{2,1,0:T(8,128)(2,1)S(1)}, u32[]{:S(2)}) copy-start(bf16[16,64,256]{2,1,0:T(8,128)(2,1)S(1)} %get-tuple-element.12) | copy-start | bytes 1572868
  15.0 551.0 %copy-start.39 = (f32[512]{0:T(512)S(1)}, f32[512]{0:T(512)}, u32[]{:S(2)}) copy-start(f32[512]{0:T(512)} %param.11) | copy-start | bytes 6148
  15.0 97.8 %collective-permute-start = (bf16[16,64,256]{2,1,0:T(8,128)(2,1)S(1)}, bf16[16,64,256]{2,1,0:T(8,128)(2,1)S(1)}, u32[]{:S(2)}, u32[]{:S(2)}) collective-permute-start(bf16[16,64,256]{2,1,0:T(8,128)(2,1)S(1)} %get-tuple-element.9), channel_id=1, source_target_pairs={{0,4},{4,8},{8,12},{12,16},{16,20},{20,24},{24,28},{28,0},{1,5},{5... | collective-permute-start | bytes 1572872 | tf_op jit(solution)/shard_map/ppermute | solution.py:16
  18.0 104.5 %collective-permute-start.1 = (bf16[16,64,256]{2,1,0:T(8,128)(2,1)S(1)}, bf16[16,64,256]{2,1,0:T(8,128)(2,1)S(1)}, u32[]{:S(2)}, u32[]{:S(2)}) collective-permute-start(bf16[16,64,256]{2,1,0:T(8,128)(2,1)S(1)} %get-tuple-element.9), channel_id=1, source_target_pairs={{0,28},{4,0},{8,4},{12,8},{16,12},{20,16},{24,20},{28,24},{1,29},{... | collective-permute-start | bytes 1572872 | tf_op jit(solution)/shard_map/ppermute | solution.py:21
  21.1 136.7 %collective-permute-start.7 = (bf16[16,64,256]{2,1,0:T(8,128)(2,1)S(1)}, bf16[16,64,256]{2,1,0:T(8,128)(2,1)S(1)}, u32[]{:S(2)}, u32[]{:S(2)}) collective-permute-start(bf16[16,64,256]{2,1,0:T(8,128)(2,1)S(1)} %get-tuple-element.10), channel_id=1, source_target_pairs={{0,4},{4,8},{8,12},{12,16},{16,20},{20,24},{24,28},{28,0},{1,5},{5... | collective-permute-start | bytes 1572872 | tf_op jit(solution)/shard_map/ppermute | solution.py:16
  21.1 146.4 %collective-permute-start.8 = (bf16[16,64,256]{2,1,0:T(8,128)(2,1)S(1)}, bf16[16,64,256]{2,1,0:T(8,128)(2,1)S(1)}, u32[]{:S(2)}, u32[]{:S(2)}) collective-permute-start(bf16[16,64,256]{2,1,0:T(8,128)(2,1)S(1)} %get-tuple-element.10), channel_id=1, source_target_pairs={{0,28},{4,0},{8,4},{12,8},{16,12},{20,16},{24,20},{28,24},{1,29},{... | collective-permute-start | bytes 1572872 | tf_op jit(solution)/shard_map/ppermute | solution.py:21
  25.9 176.9 %collective-permute-start.14 = (bf16[16,64,256]{2,1,0:T(8,128)(2,1)S(1)}, bf16[16,64,256]{2,1,0:T(8,128)(2,1)S(1)}, u32[]{:S(2)}, u32[]{:S(2)}) collective-permute-start(bf16[16,64,256]{2,1,0:T(8,128)(2,1)S(1)} %get-tuple-element.12), channel_id=1, source_target_pairs={{0,4},{4,8},{8,12},{12,16},{16,20},{20,24},{24,28},{28,0},{1,5},{5... | collective-permute-start | bytes 1572872 | tf_op jit(solution)/shard_map/ppermute | solution.py:16
  112.9 279.4 %copy-start.14 = (bf16[16,64,256]{2,1,0:T(8,128)(2,1)}, bf16[16,64,256]{2,1,0:T(8,128)(2,1)S(1)}, u32[]{:S(2)}) copy-start(bf16[16,64,256]{2,1,0:T(8,128)(2,1)S(1)} %collective-permute-done) | copy-start | bytes 1572868
  112.9 99.6 %collective-permute-start.15 = (bf16[16,64,256]{2,1,0:T(8,128)(2,1)S(1)}, bf16[16,64,256]{2,1,0:T(8,128)(2,1)S(1)}, u32[]{:S(2)}, u32[]{:S(2)}) collective-permute-start(bf16[16,64,256]{2,1,0:T(8,128)(2,1)S(1)} %get-tuple-element.12), channel_id=1, source_target_pairs={{0,28},{4,0},{8,4},{12,8},{16,12},{20,16},{24,20},{28,24},{1,29},{... | collective-permute-start | bytes 1572872 | tf_op jit(solution)/shard_map/ppermute | solution.py:21
  122.6 441.5 %copy-start.6 = (bf16[16,64,256]{2,1,0:T(8,128)(2,1)}, bf16[16,64,256]{2,1,0:T(8,128)(2,1)S(1)}, u32[]{:S(2)}) copy-start(bf16[16,64,256]{2,1,0:T(8,128)(2,1)S(1)} %collective-permute-done.1) | copy-start | bytes 1572868
  122.6 125.1 %collective-permute-start.21 = (bf16[16,64,256]{2,1,0:T(8,128)(2,1)S(1)}, bf16[16,64,256]{2,1,0:T(8,128)(2,1)S(1)}, u32[]{:S(2)}, u32[]{:S(2)}) collective-permute-start(bf16[16,64,256]{2,1,0:T(8,128)(2,1)S(1)} %get-tuple-element.11), channel_id=1, source_target_pairs={{0,4},{4,8},{8,12},{12,16},{16,20},{20,24},{24,28},{28,0},{1,5},{5... | collective-permute-start | bytes 1572872 | tf_op jit(solution)/shard_map/ppermute | solution.py:16
  157.8 354.0 %copy-start.22 = (bf16[16,64,256]{2,1,0:T(8,128)(2,1)}, bf16[16,64,256]{2,1,0:T(8,128)(2,1)S(1)}, u32[]{:S(2)}) copy-start(bf16[16,64,256]{2,1,0:T(8,128)(2,1)S(1)} %collective-permute-done.7) | copy-start | bytes 1572868
  157.8 99.6 %collective-permute-start.22 = (bf16[16,64,256]{2,1,0:T(8,128)(2,1)S(1)}, bf16[16,64,256]{2,1,0:T(8,128)(2,1)S(1)}, u32[]{:S(2)}, u32[]{:S(2)}) collective-permute-start(bf16[16,64,256]{2,1,0:T(8,128)(2,1)S(1)} %get-tuple-element.11), channel_id=1, source_target_pairs={{0,28},{4,0},{8,4},{12,8},{16,12},{20,16},{24,20},{28,24},{1,29},{... | collective-permute-start | bytes 1572872 | tf_op jit(solution)/shard_map/ppermute | solution.py:21
  167.5 215.0 %copy-start.10 = (bf16[16,64,256]{2,1,0:T(8,128)(2,1)}, bf16[16,64,256]{2,1,0:T(8,128)(2,1)S(1)}, u32[]{:S(2)}) copy-start(bf16[16,64,256]{2,1,0:T(8,128)(2,1)S(1)} %collective-permute-done.8) | copy-start | bytes 1572868
  167.5 125.1 %collective-permute-start.2 = (bf16[16,64,256]{2,1,0:T(8,128)(2,1)S(1)}, bf16[16,64,256]{2,1,0:T(8,128)(2,1)S(1)}, u32[]{:S(2)}, u32[]{:S(2)}) collective-permute-start(bf16[16,64,256]{2,1,0:T(8,128)(2,1)S(1)} %collective-permute-done), channel_id=1, source_target_pairs={{0,4},{4,8},{8,12},{12,16},{16,20},{20,24},{24,28},{28,0},{1,5},{5... | collective-permute-start | bytes 1572872 | tf_op jit(solution)/shard_map/ppermute | solution.py:16
  202.8 99.6 %collective-permute-start.3 = (bf16[16,64,256]{2,1,0:T(8,128)(2,1)S(1)}, bf16[16,64,256]{2,1,0:T(8,128)(2,1)S(1)}, u32[]{:S(2)}, u32[]{:S(2)}) collective-permute-start(bf16[16,64,256]{2,1,0:T(8,128)(2,1)S(1)} %collective-permute-done.1), channel_id=1, source_target_pairs={{0,28},{4,0},{8,4},{12,8},{16,12},{20,16},{24,20},{28,24},{1,29},{... | collective-permute-start | bytes 1572872 | tf_op jit(solution)/shard_map/ppermute | solution.py:21
  212.4 125.1 %collective-permute-start.9 = (bf16[16,64,256]{2,1,0:T(8,128)(2,1)S(1)}, bf16[16,64,256]{2,1,0:T(8,128)(2,1)S(1)}, u32[]{:S(2)}, u32[]{:S(2)}) collective-permute-start(bf16[16,64,256]{2,1,0:T(8,128)(2,1)S(1)} %collective-permute-done.7), channel_id=1, source_target_pairs={{0,4},{4,8},{8,12},{12,16},{16,20},{20,24},{24,28},{28,0},{1,5},{5... | collective-permute-start | bytes 1572872 | tf_op jit(solution)/shard_map/ppermute | solution.py:16
  247.7 234.4 %copy-start.18 = (bf16[16,64,256]{2,1,0:T(8,128)(2,1)}, bf16[16,64,256]{2,1,0:T(8,128)(2,1)S(1)}, u32[]{:S(2)}) copy-start(bf16[16,64,256]{2,1,0:T(8,128)(2,1)S(1)} %collective-permute-done.21) | copy-start | bytes 1572868
  247.7 99.6 %collective-permute-start.10 = (bf16[16,64,256]{2,1,0:T(8,128)(2,1)S(1)}, bf16[16,64,256]{2,1,0:T(8,128)(2,1)S(1)}, u32[]{:S(2)}, u32[]{:S(2)}) collective-permute-start(bf16[16,64,256]{2,1,0:T(8,128)(2,1)S(1)} %collective-permute-done.8), channel_id=1, source_target_pairs={{0,28},{4,0},{8,4},{12,8},{16,12},{20,16},{24,20},{28,24},{1,29},{... | collective-permute-start | bytes 1572872 | tf_op jit(solution)/shard_map/ppermute | solution.py:21
  257.4 224.7 %copy-start.20 = (bf16[16,64,256]{2,1,0:T(8,128)(2,1)}, bf16[16,64,256]{2,1,0:T(8,128)(2,1)S(1)}, u32[]{:S(2)}) copy-start(bf16[16,64,256]{2,1,0:T(8,128)(2,1)S(1)} %collective-permute-done.22) | copy-start | bytes 1572868
  257.4 125.1 %collective-permute-start.16 = (bf16[16,64,256]{2,1,0:T(8,128)(2,1)S(1)}, bf16[16,64,256]{2,1,0:T(8,128)(2,1)S(1)}, u32[]{:S(2)}, u32[]{:S(2)}) collective-permute-start(bf16[16,64,256]{2,1,0:T(8,128)(2,1)S(1)} %collective-permute-done.14), channel_id=1, source_target_pairs={{0,4},{4,8},{8,12},{12,16},{16,20},{20,24},{24,28},{28,0},{1,5},{5... | collective-permute-start | bytes 1572872 | tf_op jit(solution)/shard_map/ppermute | solution.py:16
  257.4 306.6 %copy-start.5 = (bf16[16,64,256]{2,1,0:T(8,128)(2,1)S(1)}, bf16[16,64,256]{2,1,0:T(8,128)(2,1)}, u32[]{:S(2)}) copy-start(bf16[16,64,256]{2,1,0:T(8,128)(2,1)} %copy-done.4) | copy-start | bytes 1572868
  292.6 224.6 %copy-start.24 = (bf16[16,64,256]{2,1,0:T(8,128)(2,1)}, bf16[16,64,256]{2,1,0:T(8,128)(2,1)S(1)}, u32[]{:S(2)}) copy-start(bf16[16,64,256]{2,1,0:T(8,128)(2,1)S(1)} %collective-permute-done.2) | copy-start | bytes 1572868
  292.6 99.7 %collective-permute-start.17 = (bf16[16,64,256]{2,1,0:T(8,128)(2,1)S(1)}, bf16[16,64,256]{2,1,0:T(8,128)(2,1)}, u32[]{:S(2)}, u32[]{:S(2)}) collective-permute-start(bf16[16,64,256]{2,1,0:T(8,128)(2,1)S(1)} %collective-permute-done.15), channel_id=1, source_target_pairs={{0,28},{4,0},{8,4},{12,8},{16,12},{20,16},{24,20},{28,24},{1,29},{... | collective-permute-start | bytes 1572872 | tf_op jit(solution)/shard_map/ppermute | solution.py:21
  302.3 125.1 %collective-permute-start.23 = (bf16[16,64,256]{2,1,0:T(8,128)(2,1)S(1)}, bf16[16,64,256]{2,1,0:T(8,128)(2,1)}, u32[]{:S(2)}, u32[]{:S(2)}) collective-permute-start(bf16[16,64,256]{2,1,0:T(8,128)(2,1)S(1)} %collective-permute-done.21), channel_id=1, source_target_pairs={{0,4},{4,8},{8,12},{12,16},{16,20},{20,24},{24,28},{28,0},{1,5},{5... | collective-permute-start | bytes 1572872 | tf_op jit(solution)/shard_map/ppermute | solution.py:16
  337.6 224.5 %copy-start.30 = (bf16[16,64,256]{2,1,0:T(8,128)(2,1)}, bf16[16,64,256]{2,1,0:T(8,128)(2,1)S(1)}, u32[]{:S(2)}) copy-start(bf16[16,64,256]{2,1,0:T(8,128)(2,1)S(1)} %collective-permute-done.9) | copy-start | bytes 1572868
  337.6 99.7 %collective-permute-start.24 = (bf16[16,64,256]{2,1,0:T(8,128)(2,1)S(1)}, bf16[16,64,256]{2,1,0:T(8,128)(2,1)}, u32[]{:S(2)}, u32[]{:S(2)}) collective-permute-start(bf16[16,64,256]{2,1,0:T(8,128)(2,1)S(1)} %collective-permute-done.22), channel_id=1, source_target_pairs={{0,28},{4,0},{8,4},{12,8},{16,12},{20,16},{24,20},{28,24},{1,29},{... | collective-permute-start | bytes 1572872 | tf_op jit(solution)/shard_map/ppermute | solution.py:21
  347.3 179.8 %copy-start.26 = (bf16[16,64,256]{2,1,0:T(8,128)(2,1)}, bf16[16,64,256]{2,1,0:T(8,128)(2,1)S(1)}, u32[]{:S(2)}) copy-start(bf16[16,64,256]{2,1,0:T(8,128)(2,1)S(1)} %collective-permute-done.10) | copy-start | bytes 1572868
  347.3 119.6 %collective-permute-start.4 = (bf16[16,64,256]{2,1,0:T(8,128)(2,1)S(1)}, bf16[16,64,256]{2,1,0:T(8,128)(2,1)}, u32[]{:S(2)}, u32[]{:S(2)}) collective-permute-start(bf16[16,64,256]{2,1,0:T(8,128)(2,1)S(1)} %collective-permute-done.2), channel_id=1, source_target_pairs={{0,4},{4,8},{8,12},{12,16},{16,20},{20,24},{24,28},{28,0},{1,5},{5... | collective-permute-start | bytes 1572872 | tf_op jit(solution)/shard_map/ppermute | solution.py:16
  382.5 179.6 %copy-start.28 = (bf16[16,64,256]{2,1,0:T(8,128)(2,1)}, bf16[16,64,256]{2,1,0:T(8,128)(2,1)S(1)}, u32[]{:S(2)}) copy-start(bf16[16,64,256]{2,1,0:T(8,128)(2,1)S(1)} %collective-permute-done.16) | copy-start | bytes 1572868
  382.5 99.6 %collective-permute-start.5 = (bf16[16,64,256]{2,1,0:T(8,128)(2,1)S(1)}, bf16[16,64,256]{2,1,0:T(8,128)(2,1)S(1)}, u32[]{:S(2)}, u32[]{:S(2)}) collective-permute-start(bf16[16,64,256]{2,1,0:T(8,128)(2,1)S(1)} %collective-permute-done.3), channel_id=1, source_target_pairs={{0,28},{4,0},{8,4},{12,8},{16,12},{20,16},{24,20},{28,24},{1,29},{... | collective-permute-start | bytes 1572872 | tf_op jit(solution)/shard_map/ppermute | solution.py:21
  392.3 119.5 %collective-permute-start.11 = (bf16[16,64,256]{2,1,0:T(8,128)(2,1)S(1)}, bf16[16,64,256]{2,1,0:T(8,128)(2,1)}, u32[]{:S(2)}, u32[]{:S(2)}) collective-permute-start(bf16[16,64,256]{2,1,0:T(8,128)(2,1)S(1)} %collective-permute-done.9), channel_id=1, source_target_pairs={{0,4},{4,8},{8,12},{12,16},{16,20},{20,24},{24,28},{28,0},{1,5},{5... | collective-permute-start | bytes 1572872 | tf_op jit(solution)/shard_map/ppermute | solution.py:16
  427.5 99.6 %collective-permute-start.12 = (bf16[16,64,256]{2,1,0:T(8,128)(2,1)S(1)}, bf16[16,64,256]{2,1,0:T(8,128)(2,1)S(1)}, u32[]{:S(2)}, u32[]{:S(2)}) collective-permute-start(bf16[16,64,256]{2,1,0:T(8,128)(2,1)S(1)} %collective-permute-done.10), channel_id=1, source_target_pairs={{0,28},{4,0},{8,4},{12,8},{16,12},{20,16},{24,20},{28,24},{1,29},{... | collective-permute-start | bytes 1572872 | tf_op jit(solution)/shard_map/ppermute | solution.py:21
  437.3 122.0 %collective-permute-start.18 = (bf16[16,64,256]{2,1,0:T(8,128)(2,1)S(1)}, bf16[16,64,256]{2,1,0:T(8,128)(2,1)}, u32[]{:S(2)}, u32[]{:S(2)}) collective-permute-start(bf16[16,64,256]{2,1,0:T(8,128)(2,1)S(1)} %collective-permute-done.16), channel_id=1, source_target_pairs={{0,4},{4,8},{8,12},{12,16},{16,20},{20,24},{24,28},{28,0},{1,5},{5... | collective-permute-start | bytes 1572872 | tf_op jit(solution)/shard_map/ppermute | solution.py:16
  466.8 427.1 %collective-permute-start.19 = (bf16[16,64,256]{2,1,0:T(8,128)(2,1)}, bf16[16,64,256]{2,1,0:T(8,128)(2,1)}, u32[]{:S(2)}, u32[]{:S(2)}) collective-permute-start(bf16[16,64,256]{2,1,0:T(8,128)(2,1)} %collective-permute-done.17), channel_id=1, source_target_pairs={{0,28},{4,0},{8,4},{12,8},{16,12},{20,16},{24,20},{28,24},{1,29},{... | collective-permute-start | bytes 1572872 | tf_op jit(solution)/shard_map/ppermute | solution.py:21
  482.1 425.6 %collective-permute-start.25 = (bf16[16,64,256]{2,1,0:T(8,128)(2,1)}, bf16[16,64,256]{2,1,0:T(8,128)(2,1)}, u32[]{:S(2)}, u32[]{:S(2)}) collective-permute-start(bf16[16,64,256]{2,1,0:T(8,128)(2,1)} %collective-permute-done.23), channel_id=1, source_target_pairs={{0,4},{4,8},{8,12},{12,16},{16,20},{20,24},{24,28},{28,0},{1,5},{5... | collective-permute-start | bytes 1572872 | tf_op jit(solution)/shard_map/ppermute | solution.py:16
  511.8 409.7 %collective-permute-start.26 = (bf16[16,64,256]{2,1,0:T(8,128)(2,1)}, bf16[16,64,256]{2,1,0:T(8,128)(2,1)}, u32[]{:S(2)}, u32[]{:S(2)}) collective-permute-start(bf16[16,64,256]{2,1,0:T(8,128)(2,1)} %collective-permute-done.24), channel_id=1, source_target_pairs={{0,28},{4,0},{8,4},{12,8},{16,12},{20,16},{24,20},{28,24},{1,29},{... | collective-permute-start | bytes 1572872 | tf_op jit(solution)/shard_map/ppermute | solution.py:21
  527.8 414.0 %collective-permute-start.6 = (bf16[16,64,256]{2,1,0:T(8,128)(2,1)}, bf16[16,64,256]{2,1,0:T(8,128)(2,1)}, u32[]{:S(2)}, u32[]{:S(2)}) collective-permute-start(bf16[16,64,256]{2,1,0:T(8,128)(2,1)} %collective-permute-done.4), channel_id=1, source_target_pairs={{0,4},{4,8},{8,12},{12,16},{16,20},{20,24},{24,28},{28,0},{1,5},{5... | collective-permute-start | bytes 1572872 | tf_op jit(solution)/shard_map/ppermute | solution.py:16
  527.8 113.6 %all-to-all-start = ((bf16[16,64,128]{2,1,0:T(8,128)(2,1)}), bf16[16,64,128]{2,1,0:T(8,128)(2,1)S(1)}, u32[]{:S(2)}, u32[]{:S(2)}) async-start(bf16[16,64,128]{2,1,0:T(8,128)(2,1)} %param.6), calls=%async_computation | async-start | bytes 524288 | tf_op jit(solution)/shard_map/all_to_all | solution.py:33
  543.9 542.9 %reduce-scatter.5.cloned.1.call-start = ((), (), s32[]{:S(2)}) async-start(), calls=%async_computation.6 | async-start | bytes 81920 | tf_op jit(solution)/shard_map/reduce_scatter | solution.py:53
  559.3 398.0 %collective-permute-start.13 = (bf16[16,64,256]{2,1,0:T(8,128)(2,1)}, bf16[16,64,256]{2,1,0:T(8,128)(2,1)}, u32[]{:S(2)}, u32[]{:S(2)}) collective-permute-start(bf16[16,64,256]{2,1,0:T(8,128)(2,1)} %collective-permute-done.11), channel_id=1, source_target_pairs={{0,4},{4,8},{8,12},{12,16},{16,20},{20,24},{24,28},{28,0},{1,5},{5... | collective-permute-start | bytes 1572872 | tf_op jit(solution)/shard_map/ppermute | solution.py:16
  935.3 44.8 %collective-permute-start.20 = (bf16[16,64,256]{2,1,0:T(8,128)(2,1)}, bf16[16,64,256]{2,1,0:T(8,128)(2,1)}, u32[]{:S(2)}, u32[]{:S(2)}) collective-permute-start(bf16[16,64,256]{2,1,0:T(8,128)(2,1)} %collective-permute-done.18), channel_id=1, source_target_pairs={{0,4},{4,8},{8,12},{12,16},{16,20},{20,24},{24,28},{28,0},{1,5},{5... | collective-permute-start | bytes 1572872 | tf_op jit(solution)/shard_map/ppermute | solution.py:16
  935.3 65.9 %collective-permute-start.27 = (bf16[16,64,256]{2,1,0:T(8,128)(2,1)}, bf16[16,64,256]{2,1,0:T(8,128)(2,1)}, u32[]{:S(2)}, u32[]{:S(2)}) collective-permute-start(bf16[16,64,256]{2,1,0:T(8,128)(2,1)} %collective-permute-done.25), channel_id=1, source_target_pairs={{0,4},{4,8},{8,12},{12,16},{16,20},{20,24},{24,28},{28,0},{1,5},{5... | collective-permute-start | bytes 1572872 | tf_op jit(solution)/shard_map/ppermute | solution.py:16
  1038.5 48.6 %reduce-scatter.7.cloned.1.call-start = ((), (), s32[]{:S(2)}) async-start(), calls=%async_computation.7 | async-start | bytes 81920 | tf_op jit(solution)/shard_map/reduce_scatter | solution.py:53
  1054.5 54.3 %reduce-scatter.9.cloned.1.call-start = ((), (), s32[]{:S(2)}) async-start(), calls=%async_computation.8 | async-start | bytes 81920 | tf_op jit(solution)/shard_map/reduce_scatter | solution.py:53
  1070.9 59.8 %reduce-scatter.11.cloned.1.call-start = ((), (), s32[]{:S(2)}) async-start(), calls=%async_computation.9 | async-start | bytes 81920 | tf_op jit(solution)/shard_map/reduce_scatter | solution.py:53
  (27 other events, 1061.5 us)
Sparse Core Ops, SparseCore 0:
  13.3 953.9 all-gather.1
  1038.6 26.2 reduce-scatter.4
  1067.5 19.5 reduce-scatter.6
  1089.3 19.4 reduce-scatter.8
  1111.2 19.4 reduce-scatter.10
